TPU v7x, 32 devices: a whole 2x2x4 slice. The times are simulated.
32 devices in a mesh: mem: 8 (over z, x), tp: 4 (over y, core).
Axes of the slice: x: 2, y: 2, z: 4, core: 2. Of those that a mesh axis runs over, the one named last changes fastest.
Arguments:
- tokens: bfloat16 [3072, 2560], P(('mem', 'tp')), may hold values from -48 to 48
- input_weight: bfloat16 [2560, 6144], P(None, 'tp'), may hold values from -0.125 to 0.125
- output_weight: bfloat16 [2048, 2560], P('tp'), may hold values from -0.125 to 0.125
- gate_logit: float32 [16], P('tp'), may hold values from -2 to 2
- memory: bfloat16 [2, 32768, 2048], P(None, 'mem', 'tp'), may hold values from -48 to 48
- retrieved: int32 [24, 16], P('mem'), may hold values from 0 to 255, as said below
- block_home: int32 [256], replicated, may hold values from 0 to 255, as said below
Outputs:
- mixed: bfloat16 [3072, 2560], P(('mem', 'tp'))
Inputs may be any that keep to these rules, and one draw needn't show every extreme that they name: `block_home`: A permutation: each logical block names one stored block; stored block s lies with index s // 32 of mem, as its block s % 32. `retrieved`: each row names 16 different logical blocks; rows i * 3 to i * 3 + 2 are the query blocks of index i of mem. A row names at most 2 blocks held by one index of mem, and all rows of one index of mem together name at most 2 different blocks held by one index of mem.
All inputs are finite; a program needn't handle non-finite values.
Results may differ from a plain program's by a relative error of at most 0.023.
Values may be sent and summed in bfloat16 or wider, within the bound.
No kernel may reach another device: no remote copies, remote signals or barrier semaphores. Data moves between devices by JAX's collectives and lax.ppermute only.
A program may use at most 128 MiB of HBM per device.

v0:
```python
import jax
import jax.numpy as jnp
from jax import lax
from jax.sharding import PartitionSpec as P

HD = 128
BLK = 128
TOPB = 16
CAP = 2
NEG_FILL = -1e30


def from_behind(value, axis, steps):
    count = lax.axis_size(axis)
    initial, last = (max(0, -steps), min(count, count - steps))
    return lax.ppermute(value, axis, [(source, source + steps) for source in range(initial, last)])


def softmax_rows(scores, allowed):
    row_peak = jnp.max(jnp.where(allowed, scores, NEG_FILL), axis=-1, keepdims=True)
    weights = jnp.where(allowed, jnp.exp(scores - row_peak), 0.0)
    return (weights / jnp.sum(weights, axis=-1, keepdims=True)).astype(jnp.bfloat16)


def local(tokens, input_weight, output_weight, gate_logit, memory, retrieved, block_home):
    holder_count = lax.axis_size("mem")
    share_rows = tokens.shape[0]
    local_rows = share_rows * lax.axis_size("tp")
    groups = output_weight.shape[0] // HD
    score_scale = HD ** (-0.5)
    projected = jnp.dot(
        lax.all_gather(tokens, "tp", axis=0, tiled=True),
        input_weight,
        preferred_element_type=jnp.float32,
    )
    projected = projected.astype(jnp.bfloat16).reshape(local_rows, groups, 3, HD)
    queries = projected[:, :, 0]
    key_rows = projected[:, :, 1]
    value_rows = projected[:, :, 2]
    last_rows = jnp.stack([key_rows[-BLK:], value_rows[-BLK:]]).reshape(2, BLK, groups * HD)
    before = from_behind(last_rows, "mem", 1).reshape(2, BLK, groups, HD)
    near_keys = jnp.concatenate([before[0], key_rows], axis=0)
    near_values = jnp.concatenate([before[1], value_rows], axis=0)
    near_scores = (
        jnp.einsum("qgd,kgd->gqk", queries, near_keys, preferred_element_type=jnp.float32)
        * score_scale
    )
    query_index = lax.broadcasted_iota(jnp.int32, (local_rows, local_rows + BLK), 0)
    key_index = lax.broadcasted_iota(jnp.int32, (local_rows, local_rows + BLK), 1)
    first_key = lax.axis_index("mem") * local_rows - BLK
    allowed = (
        (key_index > query_index) & (key_index <= query_index + BLK) & (key_index + first_key >= 0)
    )
    near_probs = softmax_rows(near_scores, allowed[None])
    near_out = jnp.einsum(
        "gqk,kgd->qgd", near_probs, near_values, preferred_element_type=jnp.float32
    )
    blocks_here = retrieved.shape[0]
    entries = blocks_here * TOPB
    local_blocks = memory.shape[1] // BLK
    flat_blocks = retrieved.reshape(entries)
    home_slot = jnp.take(block_home, flat_blocks)
    holder = home_slot // local_blocks
    local_block = home_slot % local_blocks
    local_store = memory.reshape(2, local_blocks, BLK, groups * HD)
    entry_order = jnp.arange(entries)
    earlier = entry_order[None, :] < entry_order[:, None]
    same_owner = holder[:, None] == holder[None, :]
    same_block = home_slot[:, None] == home_slot[None, :]
    first = jnp.sum(same_block & earlier, axis=1) == 0
    first_entry = jnp.argmax(same_block, axis=1)
    before_first = entry_order[None, :] < first_entry[:, None]
    slot_of = jnp.sum(same_owner & before_first & first[None, :], axis=1)
    wanted_ids = jnp.zeros((holder_count, CAP), jnp.int32).at[holder, slot_of].set(local_block)
    picked = jnp.take(
        local_store,
        lax.all_to_all(wanted_ids, "mem", split_axis=0, concat_axis=0, tiled=True).reshape(
            holder_count * CAP
        ),
        axis=1,
    )
    fetched = lax.all_to_all(picked, "mem", split_axis=1, concat_axis=1, tiled=True)
    pool = holder_count * CAP
    far_keys = fetched[0].reshape(pool * BLK, groups, HD)
    far_values = fetched[1].reshape(pool * BLK, groups, HD)
    row_of = entry_order // TOPB
    member = jnp.zeros((blocks_here, pool), jnp.bool_).at[row_of, holder * CAP + slot_of].set(True)
    far_allowed = jnp.repeat(member, BLK, axis=1)[:, None, None, :]
    block_queries = queries.reshape(blocks_here, BLK, groups, HD)
    far_scores = (
        jnp.einsum("bqgd,kgd->bgqk", block_queries, far_keys, preferred_element_type=jnp.float32)
        * score_scale
    )
    far_probs = softmax_rows(far_scores, far_allowed)
    far_out = jnp.einsum(
        "bgqk,kgd->bqgd", far_probs, far_values, preferred_element_type=jnp.float32
    )
    far_out = far_out.reshape(local_rows, groups, HD)
    mixing = jax.nn.sigmoid(gate_logit)[None, :, None]
    attended = (
        (mixing * far_out + (1.0 - mixing) * near_out)
        .astype(jnp.bfloat16)
        .reshape(local_rows, groups * HD)
    )
    return lax.psum_scatter(
        jnp.dot(attended, output_weight, preferred_element_type=jnp.float32).astype(jnp.bfloat16),
        "tp",
        scatter_dimension=0,
        tiled=True,
    )


def solution(mesh):
    placed = (
        P(("mem", "tp"), None),
        P(None, "tp"),
        P("tp", None),
        P("tp"),
        P(None, "mem", "tp"),
        P("mem", None),
        P(),
    )
    return jax.shard_map(
        local, mesh=mesh, in_specs=placed, out_specs=P(("mem", "tp"), None), check_vma=False
    )
```

profile of v0, /device:TPU:0, one launch (start us, length us, event | category | flops | bytes accessed | tf_op | source)
XLA Modules:
  0.0 221.5 jit_solution(2529680987774456837)
XLA Ops:
  6.5 0.9 reshape.393
  7.4 0.8 reshape.394
  8.2 1.5 gather_fusion
  9.7 0.7 compare_reduce_fusion
  10.4 0.2 convert_reduce_fusion.1
  10.6 0.2 convert_reduce_fusion
  10.9 2.8 %scatter_fusion = s32[8,2]{0,1:T(2,128)S(1)} fusion(s32[8,2]{0,1:T(2,128)S(1)} %broadcast.458, s32[48]{0:T(128)S(1)} %fusion.41, s32[48]{0:T(128)S(1)} %get-tuple-element.11), kind=kCustom, calls=%fused_computation.2 | custom fusion | bytes 960 | tf_op jit(solution)/shard_map/scatter | solution.py:74
  13.6 0.1 copy.53
  13.7 13.5 %all_to_all.14 = s32[8,1,2]{2,1,0:T(1,128)S(1)} all-to-all(s32[8,1,2]{2,1,0:T(1,128)S(1)} %copy.53), channel_id=1, replica_groups=mesh['mem'=8,'tp'=4] {'mem'}, dimensions={0} | all-to-all | bytes 128 | tf_op jit(solution)/shard_map/all_to_all | solution.py:77
  27.2 0.1 reshape.397
  27.3 0.5 broadcast.518
  27.8 0.7 reduce.24
  28.5 0.1 reshape.395
  28.6 6.2 %gather_fusion.1 = bf16[16,2,128,512]{3,2,1,0:T(8,128)(2,1)} fusion(bf16[2,32,128,512]{3,2,1,0:T(8,128)(2,1)} %bitcast.89, s32[1024]{0:T(1024)S(1)} %pad_clamp_fusion), kind=kCustom, calls=%fused_computation.1 | custom fusion | bytes 8388672 | tf_op jit(solution)/shard_map/jit(_take)/gather | solution.py:75
  34.7 4.6 %select_bitcast_fusion = bf16[2,16,128,512]{3,2,0,1:T(8,128)(2,1)} fusion(bf16[16,2,128,512]{3,2,1,0:T(8,128)(2,1)} %gather_fusion.1, pred[16]{0:T(512)(128)(4,1)S(1)} %compare_and_fusion.1), kind=kLoop, calls=%fused_computation.18 | loop fusion | flops 2097152 | bytes 8388624 | tf_op jit(solution)/shard_map/jit(_take)/select_n | solution.py:75
  39.4 4.5 %all-to-all-start.1 = ((bf16[2,16,128,512]{3,2,0,1:T(8,128)(2,1)}), bf16[2,16,128,512]{3,2,0,1:T(8,128)(2,1)}, u32[]{:S(2)}, u32[]{:S(2)}) async-start(bf16[2,16,128,512]{3,2,0,1:T(8,128)(2,1)} %select_bitcast_fusion), calls=%async_computation.1 | async-start | bytes 8388608 | tf_op jit(solution)/shard_map/all_to_all | solution.py:82
  43.9 0.0 all-gather.2.cloned.1.call-start
  44.0 0.7 all-gather.2.cloned.1.call-update
  44.7 0.0 reduce-scatter.2.cloned.1.call-start
  44.7 2.8 %scatter_fusion.1 = pred[3,16]{1,0:T(4,128)(4,1)S(1)} fusion(pred[3,16]{1,0:T(4,128)(4,1)S(1)} %broadcast_in_dim.88, s32[48]{0:T(128)S(1)} %get-tuple-element.9, pred[48]{0:T(512)(128)(4,1)S(1)} %broadcast.492), kind=kCustom, calls=%fused_computation.3 | custom fusion | bytes 528 | tf_op jit(solution)/shard_map/scatter | solution.py:87
  47.6 0.1 broadcast_bitcast_fusion
  47.7 0.9 fusion.26
  48.5 21.0 %all-gather.2.cloned.1.call-done = bf16[384,2560]{1,0:T(8,128)(2,1)} async-done(((bf16[96,2560]{1,0:T(8,128)(2,1)}), bf16[384,2560]{1,0:T(8,128)(2,1)}) %all-gather.2.cloned.1.call-update) | async-done | bytes 1966096 | tf_op jit(solution)/shard_map/all_gather | solution.py:32
  69.5 8.1 %convolution_convert_fusion.1 = bf16[384,1536]{1,0:T(8,128)(2,1)} fusion(bf16[384,2560]{1,0:T(8,128)(2,1)} %all-gather.2.cloned.1.call-done, bf16[2560,1536]{1,0:T(8,128)(2,1)} %param.8), kind=kOutput, calls=%fused_computation.23 | convolution fusion | flops 3020488704 | bytes 11010048 | tf_op jit(solution)/shard_map/dot_general | solution.py:31
  77.6 2.4 %copy.56 = bf16[384,1536]{0,1:T(8,128)(2,1)} copy(bf16[384,1536]{1,0:T(8,128)(2,1)} %convolution_convert_fusion.1) | data formatting | bytes 2359296 | tf_op jit(solution)/shard_map/convert_element_type | solution.py:36
  80.0 1.0 fusion.51
  81.0 0.7 pad_maximum_fusion
  81.8 4.1 %collective-permute-start = (bf16[2,128,512]{1,2,0:T(8,128)(2,1)}, bf16[2,128,512]{1,2,0:T(8,128)(2,1)}, u32[]{:S(2)}, u32[]{:S(2)}) collective-permute-start(bf16[2,128,512]{1,2,0:T(8,128)(2,1)} %pad_maximum_fusion), channel_id=1, source_target_pairs={{0,4},{4,8},{8,12},{12,16},{16,20},{20,24},{24,28},{1,5},{5,9},{9,... | collective-permute-start | bytes 786440 | tf_op jit(solution)/shard_map/ppermute | solution.py:16
  85.9 2.1 slice_bitcast_fusion
  88.0 0.9 copy.76
  88.9 0.2 copy.78
  89.2 2.2 %collective-permute-done = bf16[2,128,512]{1,2,0:T(8,128)(2,1)} collective-permute-done((bf16[2,128,512]{1,2,0:T(8,128)(2,1)}, bf16[2,128,512]{1,2,0:T(8,128)(2,1)}, u32[]{:S(2)}, u32[]{:S(2)}) %collective-permute-start) | collective-permute-done | bytes 262176 | tf_op jit(solution)/shard_map/ppermute | solution.py:16
  91.4 1.0 fusion.52
  92.4 0.1 copy.64
  92.5 1.7 fusion.30
  94.2 3.7 %fusion.53 = (f32[4,384]{1,0:T(4,128)}, f32[4,384,512]{2,1,0:T(8,128)}) fusion(f32[4,384,512]{2,1,0:T(8,128)S(1)} %fusion.30, pred[384,512]{1,0:T(8,128)(4,1)S(1)} %copy-done.3), kind=kOutput, calls=%fused_computation.114 | output fusion | flops 4719103 | bytes 6494208 | tf_op jit(solution)/shard_map/sub | solution.py:21
  97.9 38.0 %all-to-all-done.1 = bf16[2,16,128,512]{3,2,0,1:T(8,128)(2,1)} async-done(((bf16[2,16,128,512]{3,2,0,1:T(8,128)(2,1)}), bf16[2,16,128,512]{3,2,0,1:T(8,128)(2,1)}, u32[]{:S(2)}, u32[]{:S(2)}) %all-to-all-start.1) | async-done | bytes 4194336 | tf_op jit(solution)/shard_map/all_to_all | solution.py:82
  135.9 4.6 %fusion.50 = (bf16[1,16,128,512]{3,2,0,1:T(8,128)(2,1)}, bf16[1,16,128,512]{3,2,0,1:T(8,128)(2,1)}) fusion(bf16[2,16,128,512]{3,2,0,1:T(8,128)(2,1)} %all-to-all-done.1), kind=kLoop, calls=%fused_computation.111 | loop fusion | bytes 8388608 | tf_op jit(solution)/shard_map/slice | solution.py:85
  140.6 4.0 %reshape.432 = bf16[2048,4,128]{2,1,0:T(4,128)(2,1)} reshape(bf16[1,16,128,512]{3,2,0,1:T(8,128)(2,1)} %get-tuple-element.14) | data formatting | bytes 4194304 | tf_op jit(solution)/shard_map/reshape;squeeze | solution.py:84
  144.5 4.0 %reshape.431 = bf16[2048,4,128]{2,1,0:T(4,128)(2,1)} reshape(bf16[1,16,128,512]{3,2,0,1:T(8,128)(2,1)} %get-tuple-element.13) | data formatting | bytes 4194304 | tf_op jit(solution)/shard_map/reshape;squeeze | solution.py:85
  148.6 3.4 %fusion.14 = f32[4,2048,3,128]{3,1,2,0:T(8,128)S(1)} fusion(bf16[3,128,4,128]{3,1,0,2:T(8,128)(2,1)S(1)} %bitcast.91, bf16[2048,4,128,1]{2,1,0,3:T(4,128)(2,1)} %bitcast.85), kind=kOutput, calls=%fused_computation.25 | convolution fusion | flops 805306368 | bytes 15073280 | tf_op jit(solution)/shard_map/bqgd,kgd->bgqk/dot_general | solution.py:91
  152.0 6.9 %fusion.54 = (f32[3,4,128]{2,0,1:T(4,128)S(1)}, f32[3,4,128,2048]{2,3,0,1:T(8,128)}) fusion(f32[4,2048,3,128]{3,1,2,0:T(8,128)S(1)} %fusion.14, pred[3,2048]{1,0:T(4,128)(4,1)S(1)} %bitcast.100), kind=kOutput, calls=%fused_computation.115 | output fusion | flops 18876416 | bytes 25178112 | tf_op jit(solution)/shard_map/sub | solution.py:21
  158.9 7.9 %fusion.9 = f32[4,128,3,128]{1,3,2,0:T(8,128)} fusion(f32[3,4,128,2048]{2,3,0,1:T(8,128)} %get-tuple-element.25, f32[3,4,128]{2,0,1:T(4,128)S(1)} %get-tuple-element.24, bf16[2048,4,128,1]{2,1,0,3:T(4,128)(2,1)S(1)} %bitcast.90), kind=kOutput, calls=%fused_computation.16 | convolution fusion | flops 811597824 | bytes 15472640 | tf_op jit(solution)/shard_map/bgqk,kgd->bqgd/dot_general | solution.py:95
  166.8 1.4 copy.61
  168.2 2.7 %fusion.24 = bf16[384,4,128]{0,2,1:T(8,128)(2,1)S(1)} fusion(f32[4,384,512]{2,1,0:T(8,128)} %get-tuple-element.23, f32[4,384]{1,0:T(4,128)S(1)} %copy-done.5, f32[384,4,128]{0,2,1:T(8,128)S(1)} %copy.61, bf16[384,4,128]{0,2,1:T(8,128)(2,1)} %get-tuple-element.15, bf16[128,4,128]{0,2,1:T(8,128)(2,1)S(1)} %bitcast.98, f32[4]{0:T(128)S(1)} %get-tuple-element.7, ...), kind=kOutput, calls=%fused_computation.35 | convolution fusion | flops 204734464 | bytes 4855840 | tf_op jit(solution)/shard_map/gqk,kgd->qgd/dot_general | solution.py:55
  171.0 2.5 %convolution_convert_fusion = bf16[384,2560]{1,0:T(8,128)(2,1)} fusion(bf16[384,512]{0,1:T(8,128)(2,1)S(1)} %bitcast.97, bf16[512,2560]{1,0:T(8,128)(2,1)S(1)} %copy-done), kind=kOutput, calls=%fused_computation.17 | convolution fusion | flops 1007616000 | bytes 4980736 | tf_op jit(solution)/shard_map/dot_general | solution.py:106
  173.5 0.0 reduce-scatter.2.cloned.1.call-update
  173.5 41.1 %reduce-scatter.2.cloned.1.call-done = bf16[96,2560]{1,0:T(8,128)(2,1)} async-done(((bf16[384,2560]{1,0:T(8,128)(2,1)}), bf16[96,2560]{1,0:T(8,128)(2,1)}) %reduce-scatter.2.cloned.1.call-update) | async-done | bytes 491536 | tf_op jit(solution)/shard_map/reduce_scatter | solution.py:105
  (29 shorter events, 0.2 us)
Async XLA Ops:
  6.5 164.4 %copy-start = (bf16[512,2560]{1,0:T(8,128)(2,1)S(1)}, bf16[512,2560]{1,0:T(8,128)(2,1)}, u32[]{:S(2)}) copy-start(bf16[512,2560]{1,0:T(8,128)(2,1)} %param.9) | copy-start | bytes 7864324
  39.4 96.6 %all-to-all-start.1 = ((bf16[2,16,128,512]{3,2,0,1:T(8,128)(2,1)}), bf16[2,16,128,512]{3,2,0,1:T(8,128)(2,1)}, u32[]{:S(2)}, u32[]{:S(2)}) async-start(bf16[2,16,128,512]{3,2,0,1:T(8,128)(2,1)} %select_bitcast_fusion), calls=%async_computation.1 | async-start | bytes 8388608 | tf_op jit(solution)/shard_map/all_to_all | solution.py:82
  43.9 25.6 %all-gather.2.cloned.1.call-start = ((), (), s32[]{:S(2)}) async-start(), calls=%async_computation.3 | async-start | bytes 2457600 | tf_op jit(solution)/shard_map/all_gather | solution.py:32
  44.7 170.0 %reduce-scatter.2.cloned.1.call-start = ((), (), s32[]{:S(2)}) async-start(), calls=%async_computation.4 | async-start | bytes 2457600 | tf_op jit(solution)/shard_map/reduce_scatter | solution.py:105
  77.6 8.3 %copy-start.4 = (f32[4]{0:T(128)S(1)}, f32[4]{0:T(128)}, u32[]{:S(2)}) copy-start(f32[4]{0:T(128)} %param.10) | copy-start | bytes 52
  81.8 9.6 %collective-permute-start = (bf16[2,128,512]{1,2,0:T(8,128)(2,1)}, bf16[2,128,512]{1,2,0:T(8,128)(2,1)}, u32[]{:S(2)}, u32[]{:S(2)}) collective-permute-start(bf16[2,128,512]{1,2,0:T(8,128)(2,1)} %pad_maximum_fusion), channel_id=1, source_target_pairs={{0,4},{4,8},{8,12},{12,16},{16,20},{20,24},{24,28},{1,5},{5,9},{9,... | collective-permute-start | bytes 786440 | tf_op jit(solution)/shard_map/ppermute | solution.py:16
  92.5 1.7 copy-start.3
  144.5 4.0 %copy-start.2 = (bf16[384,4,1,128]{3,0,1,2:T(8,128)(2,1)S(1)}, bf16[384,4,1,128]{3,0,1,2:T(8,128)(2,1)}, u32[]{:S(2)}) copy-start(bf16[384,4,1,128]{3,0,1,2:T(8,128)(2,1)} %copy.76) | copy-start | bytes 1179652
  152.0 6.9 %copy-start.1 = (bf16[2048,4,128]{2,1,0:T(4,128)(2,1)S(1)}, bf16[2048,4,128]{2,1,0:T(4,128)(2,1)}, u32[]{:S(2)}) copy-start(bf16[2048,4,128]{2,1,0:T(4,128)(2,1)} %reshape.431) | copy-start | bytes 6291460
  158.9 9.3 %copy-start.5 = (f32[4,384]{1,0:T(4,128)S(1)}, f32[4,384]{1,0:T(4,128)}, u32[]{:S(2)}) copy-start(f32[4,384]{1,0:T(4,128)} %get-tuple-element.22) | copy-start | bytes 18436
Sparse Core Ops, SparseCore 0:
  46.3 23.1 all-gather.1
  173.6 40.9 reduce-scatter.1
where the time goes:
time: 222 us; the launch traced here: 221 us
  waiting for transfers between devices  103 us (46%)
  local copies, waits for them, and re-layouts  37.6 us (17%)
  matrix products  26.2 us (12%)
  other arithmetic  18.7 us (8%)
  between operations  13.6 us (6%)
  blocking collectives  13.5 us (6%)
  starting transfers between devices  8.71 us (4%)
    reduce_scatter x1, waiting for transfers between devices, local(): lax.psum_scatter(jnp.dot(attended, output_weight, preferred_element_type=...  41.1 us
    all_to_all x1, waiting for transfers between devices, local(): lax.all_to_all(picked, 'mem', split_axis=1, concat_axis=1, tiled=True)  38 us
    all_gather x1, waiting for transfers between devices, local(): lax.all_gather(tokens, 'tp', axis=0, tiled=True)  21 us
    all_to_all x1, blocking collectives, local(): lax.all_to_all(wanted_ids, 'mem', split_axis=0, concat_axis=0, tiled=True)  13.5 us
    sub x2, other arithmetic, softmax_rows(): weights = jnp.where(allowed, jnp.exp(scores - row_peak), 0.0)  10.6 us
    dot_general x1, matrix products, local(): jnp.dot(lax.all_gather(tokens, 'tp', axis=0, tiled=True), input_weight, p...  8.05 us
    dot_general x1, matrix products, local(): jnp.einsum('bgqk,kgd->bqgd', far_probs, far_values, preferred_element_typ...  7.92 us
    gather x1, local copies, waits for them, and re-layouts, local(): jnp.take(local_store, lax.all_to_all(wanted_ids, 'mem', split_axis=0, con...  6.17 us
  transfers between devices with their start and end apart: 4, of which 4 were waited for; matrix products, arithmetic and copies ran while one was open for 12% of the time, Pallas kernels for 0%

commit v1 on v0

--- a/solution.py
+++ b/solution.py
@@ -8,6 +8,28 @@
 TOPB = 16
 CAP = 2
 NEG_FILL = -1e30
+
+
+def split_up(shard, dim, peers):
+    before, after = (shard.shape[:dim], shard.shape[dim + 1 :])
+    return jnp.moveaxis(shard.reshape(*before, peers, -1, *after), dim, 0)
+
+
+def laid_out(pieces, dim):
+    pieces = jnp.moveaxis(pieces, 0, dim)
+    dims = pieces.shape
+    return pieces.reshape(*dims[:dim], dims[dim] * dims[dim + 1], *dims[dim + 2 :])
+
+
+def exchange_in_pairs(x, axis, split_dim, concat_dim):
+    size, position = (lax.axis_size(axis), lax.axis_index(axis))
+    tiles = split_up(x, split_dim, size)
+    gathered = [tiles[position]]
+    for hop in range(1, size):
+        sent = tiles[position ^ hop]
+        gathered.append(lax.ppermute(sent, axis, [(i, i ^ hop) for i in range(size)]))
+    tiles = jnp.stack(gathered)[position ^ jnp.arange(size)]
+    return laid_out(tiles, concat_dim)
 
 
 def from_behind(value, axis, steps):
@@ -73,11 +95,7 @@
     slot_of = jnp.sum(same_owner & before_first & first[None, :], axis=1)
     wanted_ids = jnp.zeros((holder_count, CAP), jnp.int32).at[holder, slot_of].set(local_block)
     picked = jnp.take(
-        local_store,
-        lax.all_to_all(wanted_ids, "mem", split_axis=0, concat_axis=0, tiled=True).reshape(
-            holder_count * CAP
-        ),
-        axis=1,
+        local_store, exchange_in_pairs(wanted_ids, "mem", 0, 0).reshape(holder_count * CAP), axis=1
     )
     fetched = lax.all_to_all(picked, "mem", split_axis=1, concat_axis=1, tiled=True)
     pool = holder_count * CAP

time: 222 us -> 224 us (level)
  blocking collectives: 13.5 us -> 0 us
  starting transfers between devices: 8.71 us -> 21.2 us
  waiting for transfers between devices: 103 us -> 107 us
    all_to_all x1 -> x0, blocking collectives: 13.5 us -> none  [local(): lax.all_to_all(wanted_ids, 'mem', split_axis=0, concat_axis=0, tiled=True)]
    ppermute x0 -> x7, starting transfers between devices: none -> 12.5 us  [exchange_in_pairs(): lax.ppermute(sent, axis, [(i, i ^ hop) for i in range(size)])]
    ppermute x0 -> x7, waiting for transfers between devices: none -> 4.76 us  [exchange_in_pairs(): lax.ppermute(sent, axis, [(i, i ^ hop) for i in range(size)])]
    gather x1 -> x2, local copies, waits for them, and re-layouts: 6.17 us -> 6.72 us  [the longest x1 6.17 us: local(): jnp.take(local_store, exchange_in_pairs(wanted_ids, 'mem', 0, 0).reshape(...]
    select_n x2 -> x3, other arithmetic: 4.63 us -> 4.63 us  [the longest x2 4.62 us: local(): jnp.take(local_store, exchange_in_pairs(wanted_ids, 'mem', 0, 0).reshape(...]
  transfers between devices with their start and end apart: 4 -> 11, of which waited for: 4 -> 6; matrix products, arithmetic and copies ran while one was open for 12% -> 12% of each run, Pallas kernels for 0% -> 0%
where the time goes in v1:
time: 224 us
  waiting for transfers between devices  107 us (48%)
  local copies, waits for them, and re-layouts  37.9 us (17%)
  matrix products  26.2 us (12%)
  starting transfers between devices  21.2 us (9%)
  other arithmetic  18.1 us (8%)
  between operations  13.7 us (6%)
    reduce_scatter x1, waiting for transfers between devices, local(): lax.psum_scatter(jnp.dot(attended, output_weight, preferred_element_type=...  41.1 us
    all_to_all x1, waiting for transfers between devices, local(): lax.all_to_all(picked, 'mem', split_axis=1, concat_axis=1, tiled=True)  36.9 us
    all_gather x1, waiting for transfers between devices, local(): lax.all_gather(tokens, 'tp', axis=0, tiled=True)  21 us
    ppermute x7, starting transfers between devices, exchange_in_pairs(): lax.ppermute(sent, axis, [(i, i ^ hop) for i in range(size)])  12.5 us
    sub x2, other arithmetic, softmax_rows(): weights = jnp.where(allowed, jnp.exp(scores - row_peak), 0.0)  10.6 us
    dot_general x1, matrix products, local(): jnp.dot(lax.all_gather(tokens, 'tp', axis=0, tiled=True), input_weight, p...  8.05 us
    dot_general x1, matrix products, local(): jnp.einsum('bgqk,kgd->bqgd', far_probs, far_values, preferred_element_typ...  7.92 us
    gather x1, local copies, waits for them, and re-layouts, local(): jnp.take(local_store, exchange_in_pairs(wanted_ids, 'mem', 0, 0).reshape(...  6.17 us
  transfers between devices with their start and end apart: 11, of which 6 were waited for; matrix products, arithmetic and copies ran while one was open for 12% of the time, Pallas kernels for 0%

profile of v1, /device:TPU:0, one launch (start us, length us, event | category | flops | bytes accessed | tf_op | source)
XLA Modules:
  0.0 223.8 jit_solution(6233978918659090933)
XLA Ops:
  6.5 0.9 reshape.416
  7.4 0.8 reshape.417
  8.2 1.5 gather_fusion
  9.7 0.7 compare_reduce_fusion
  10.4 0.2 convert_reduce_fusion.1
  10.7 0.2 convert_reduce_fusion
  10.9 2.8 %scatter_fusion = s32[8,2]{0,1:T(2,128)S(1)} fusion(s32[8,2]{0,1:T(2,128)S(1)} %broadcast.489, s32[48]{0:T(128)S(1)} %fusion.43, s32[48]{0:T(128)S(1)} %get-tuple-element.11), kind=kCustom, calls=%fused_computation.3 | custom fusion | bytes 960 | tf_op jit(solution)/shard_map/scatter | solution.py:96
  13.8 5.1 %collective-permute-start.5 = (s32[1,2]{0,1:T(2,128)S(1)}, s32[1,2]{0,1:T(2,128)S(1)}, u32[]{:S(2)}, u32[]{:S(2)}) collective-permute-start(s32[1,2]{0,1:T(2,128)S(1)} %get-tuple-element.23), channel_id=1, source_target_pairs={{0,24},{4,28},{8,16},{12,20},{16,8},{20,12},{24,0},{28,4},{1,25},{... | collective-permute-start | bytes 32 | tf_op jit(solution)/shard_map/ppermute | solution.py:30
  18.8 1.1 collective-permute-start.6
  20.0 0.4 collective-permute-start
  20.4 3.1 %collective-permute-start.2 = (s32[1,2]{0,1:T(2,128)S(1)}, s32[1,2]{0,1:T(2,128)S(1)}, u32[]{:S(2)}, u32[]{:S(2)}) collective-permute-start(s32[1,2]{0,1:T(2,128)S(1)} %get-tuple-element.26), channel_id=1, source_target_pairs={{0,12},{4,8},{8,4},{12,0},{16,28},{20,24},{24,20},{28,16},{1,13},{... | collective-permute-start | bytes 32 | tf_op jit(solution)/shard_map/ppermute | solution.py:30
  23.5 2.2 collective-permute-start.3
  25.7 0.6 collective-permute-start.4
  26.3 1.7 collective-permute-done.3
  28.0 3.0 %collective-permute-done.4 = s32[1,2]{0,1:T(2,128)S(1)} collective-permute-done((s32[1,2]{0,1:T(2,128)S(1)}, s32[1,2]{0,1:T(2,128)S(1)}, u32[]{:S(2)}, u32[]{:S(2)}) %collective-permute-start.4) | collective-permute-done | bytes 40 | tf_op jit(solution)/shard_map/ppermute | solution.py:30
  31.1 0.1 stack.40
  31.3 0.6 gather_fusion.1
  32.0 6.2 %gather_fusion.2 = bf16[16,2,128,512]{3,2,1,0:T(8,128)(2,1)} fusion(bf16[2,32,128,512]{3,2,1,0:T(8,128)(2,1)} %bitcast.98, s32[1024]{0:T(1024)S(1)} %pad_clamp_fusion), kind=kCustom, calls=%fused_computation.2 | custom fusion | bytes 8388672 | tf_op jit(solution)/shard_map/jit(_take)/gather | solution.py:97
  38.2 4.6 %select_bitcast_fusion = bf16[2,16,128,512]{3,2,0,1:T(8,128)(2,1)} fusion(bf16[16,2,128,512]{3,2,1,0:T(8,128)(2,1)} %gather_fusion.2, pred[16]{0:T(512)(128)(4,1)S(1)} %compare_and_fusion.1), kind=kLoop, calls=%fused_computation.19 | loop fusion | flops 2097152 | bytes 8388624 | tf_op jit(solution)/shard_map/jit(_take)/select_n | solution.py:97
  42.8 4.5 %all-to-all-start = ((bf16[2,16,128,512]{3,2,0,1:T(8,128)(2,1)}), bf16[2,16,128,512]{3,2,0,1:T(8,128)(2,1)}, u32[]{:S(2)}, u32[]{:S(2)}) async-start(bf16[2,16,128,512]{3,2,0,1:T(8,128)(2,1)} %select_bitcast_fusion), calls=%async_computation | async-start | bytes 8388608 | tf_op jit(solution)/shard_map/all_to_all | solution.py:100
  47.4 0.7 all-gather.2.cloned.1.call-update
  48.2 2.8 %scatter_fusion.1 = pred[3,16]{1,0:T(4,128)(4,1)S(1)} fusion(pred[3,16]{1,0:T(4,128)(4,1)S(1)} %broadcast_in_dim.89, s32[48]{0:T(128)S(1)} %get-tuple-element.9, pred[48]{0:T(512)(128)(4,1)S(1)} %broadcast.527), kind=kCustom, calls=%fused_computation.4 | custom fusion | bytes 528 | tf_op jit(solution)/shard_map/scatter | solution.py:105
  51.1 0.9 fusion.26
  52.0 21.0 %all-gather.2.cloned.1.call-done = bf16[384,2560]{1,0:T(8,128)(2,1)} async-done(((bf16[96,2560]{1,0:T(8,128)(2,1)}), bf16[384,2560]{1,0:T(8,128)(2,1)}) %all-gather.2.cloned.1.call-update) | async-done | bytes 1966096 | tf_op jit(solution)/shard_map/all_gather | solution.py:54
  73.0 8.1 %convolution_convert_fusion.1 = bf16[384,1536]{1,0:T(8,128)(2,1)} fusion(bf16[384,2560]{1,0:T(8,128)(2,1)} %all-gather.2.cloned.1.call-done, bf16[2560,1536]{1,0:T(8,128)(2,1)} %param.8), kind=kOutput, calls=%fused_computation.24 | convolution fusion | flops 3020488704 | bytes 11010048 | tf_op jit(solution)/shard_map/dot_general | solution.py:53
  81.1 2.4 %copy.72 = bf16[384,1536]{0,1:T(8,128)(2,1)} copy(bf16[384,1536]{1,0:T(8,128)(2,1)} %convolution_convert_fusion.1) | data formatting | bytes 2359296 | tf_op jit(solution)/shard_map/convert_element_type | solution.py:58
  83.5 1.0 fusion.53
  84.5 0.7 pad_maximum_fusion
  85.2 4.1 %collective-permute-start.7 = (bf16[2,128,512]{1,2,0:T(8,128)(2,1)}, bf16[2,128,512]{1,2,0:T(8,128)(2,1)}, u32[]{:S(2)}, u32[]{:S(2)}) collective-permute-start(bf16[2,128,512]{1,2,0:T(8,128)(2,1)} %pad_maximum_fusion), channel_id=1, source_target_pairs={{0,4},{4,8},{8,12},{12,16},{16,20},{20,24},{24,28},{1,5},{5,9},{9,... | collective-permute-start | bytes 786440 | tf_op jit(solution)/shard_map/ppermute | solution.py:38
  89.3 2.1 slice_bitcast_fusion
  91.5 0.9 copy.92
  92.4 0.2 copy.94
  92.6 2.2 collective-permute-done.7
  94.8 1.0 fusion.54
  95.8 0.1 copy.80
  96.0 1.7 fusion.30
  97.7 3.7 %fusion.55 = (f32[4,384]{1,0:T(4,128)}, f32[4,384,512]{2,1,0:T(8,128)}) fusion(f32[4,384,512]{2,1,0:T(8,128)S(1)} %fusion.30, pred[384,512]{1,0:T(8,128)(4,1)S(1)} %copy-done.3), kind=kOutput, calls=%fused_computation.127 | output fusion | flops 4719103 | bytes 6494208 | tf_op jit(solution)/shard_map/sub | solution.py:43
  101.4 36.9 %all-to-all-done = bf16[2,16,128,512]{3,2,0,1:T(8,128)(2,1)} async-done(((bf16[2,16,128,512]{3,2,0,1:T(8,128)(2,1)}), bf16[2,16,128,512]{3,2,0,1:T(8,128)(2,1)}, u32[]{:S(2)}, u32[]{:S(2)}) %all-to-all-start) | async-done | bytes 4194336 | tf_op jit(solution)/shard_map/all_to_all | solution.py:100
  138.3 4.6 %fusion.52 = (bf16[1,16,128,512]{3,2,0,1:T(8,128)(2,1)}, bf16[1,16,128,512]{3,2,0,1:T(8,128)(2,1)}) fusion(bf16[2,16,128,512]{3,2,0,1:T(8,128)(2,1)} %all-to-all-done), kind=kLoop, calls=%fused_computation.124 | loop fusion | bytes 8388608 | tf_op jit(solution)/shard_map/slice | solution.py:103
  142.9 4.0 %reshape.465 = bf16[2048,4,128]{2,1,0:T(4,128)(2,1)} reshape(bf16[1,16,128,512]{3,2,0,1:T(8,128)(2,1)} %get-tuple-element.14) | data formatting | bytes 4194304 | tf_op jit(solution)/shard_map/reshape;squeeze | solution.py:102
  146.9 4.0 %reshape.464 = bf16[2048,4,128]{2,1,0:T(4,128)(2,1)} reshape(bf16[1,16,128,512]{3,2,0,1:T(8,128)(2,1)} %get-tuple-element.13) | data formatting | bytes 4194304 | tf_op jit(solution)/shard_map/reshape;squeeze | solution.py:103
  150.9 3.4 %fusion.14 = f32[4,2048,3,128]{3,1,2,0:T(8,128)S(1)} fusion(bf16[3,128,4,128]{3,1,0,2:T(8,128)(2,1)S(1)} %bitcast.100, bf16[2048,4,128,1]{2,1,0,3:T(4,128)(2,1)} %bitcast.94), kind=kOutput, calls=%fused_computation.26 | convolution fusion | flops 805306368 | bytes 15073280 | tf_op jit(solution)/shard_map/bqgd,kgd->bgqk/dot_general | solution.py:109
  154.3 6.9 %fusion.56 = (f32[3,4,128]{2,0,1:T(4,128)S(1)}, f32[3,4,128,2048]{2,3,0,1:T(8,128)}) fusion(f32[4,2048,3,128]{3,1,2,0:T(8,128)S(1)} %fusion.14, pred[3,2048]{1,0:T(4,128)(4,1)S(1)} %bitcast.108), kind=kOutput, calls=%fused_computation.128 | output fusion | flops 18876416 | bytes 25178112 | tf_op jit(solution)/shard_map/sub | solution.py:43
  161.2 7.9 %fusion.9 = f32[4,128,3,128]{1,3,2,0:T(8,128)} fusion(f32[3,4,128,2048]{2,3,0,1:T(8,128)} %get-tuple-element.33, f32[3,4,128]{2,0,1:T(4,128)S(1)} %get-tuple-element.32, bf16[2048,4,128,1]{2,1,0,3:T(4,128)(2,1)S(1)} %bitcast.99), kind=kOutput, calls=%fused_computation.17 | convolution fusion | flops 811597824 | bytes 15472640 | tf_op jit(solution)/shard_map/bgqk,kgd->bqgd/dot_general | solution.py:113
  169.1 1.4 copy.77
  170.5 2.7 %fusion.24 = bf16[384,4,128]{0,2,1:T(8,128)(2,1)S(1)} fusion(f32[4,384,512]{2,1,0:T(8,128)} %get-tuple-element.31, f32[4,384]{1,0:T(4,128)S(1)} %copy-done.5, f32[384,4,128]{0,2,1:T(8,128)S(1)} %copy.77, bf16[384,4,128]{0,2,1:T(8,128)(2,1)} %get-tuple-element.15, bf16[128,4,128]{0,2,1:T(8,128)(2,1)S(1)} %bitcast.107, f32[4]{0:T(128)S(1)} %get-tuple-element.7, ...), kind=kOutput, calls=%fused_computation.36 | convolution fusion | flops 204734464 | bytes 4855840 | tf_op jit(solution)/shard_map/gqk,kgd->qgd/dot_general | solution.py:77
  173.3 2.5 %convolution_convert_fusion = bf16[384,2560]{1,0:T(8,128)(2,1)} fusion(bf16[384,512]{0,1:T(8,128)(2,1)S(1)} %bitcast.106, bf16[512,2560]{1,0:T(8,128)(2,1)S(1)} %copy-done), kind=kOutput, calls=%fused_computation.18 | convolution fusion | flops 1007616000 | bytes 4980736 | tf_op jit(solution)/shard_map/dot_general | solution.py:124
  175.8 41.1 %reduce-scatter.2.cloned.1.call-done = bf16[96,2560]{1,0:T(8,128)(2,1)} async-done(((bf16[384,2560]{1,0:T(8,128)(2,1)}), bf16[96,2560]{1,0:T(8,128)(2,1)}) %reduce-scatter.2.cloned.1.call-update) | async-done | bytes 491536 | tf_op jit(solution)/shard_map/reduce_scatter | solution.py:123
  (45 shorter events, 0.7 us)
Async XLA Ops:
  6.5 166.8 %copy-start = (bf16[512,2560]{1,0:T(8,128)(2,1)S(1)}, bf16[512,2560]{1,0:T(8,128)(2,1)}, u32[]{:S(2)}) copy-start(bf16[512,2560]{1,0:T(8,128)(2,1)} %param.9) | copy-start | bytes 7864324
  13.8 9.7 %collective-permute-start.5 = (s32[1,2]{0,1:T(2,128)S(1)}, s32[1,2]{0,1:T(2,128)S(1)}, u32[]{:S(2)}, u32[]{:S(2)}) collective-permute-start(s32[1,2]{0,1:T(2,128)S(1)} %get-tuple-element.23), channel_id=1, source_target_pairs={{0,24},{4,28},{8,16},{12,20},{16,8},{20,12},{24,0},{28,4},{1,25},{... | collective-permute-start | bytes 32 | tf_op jit(solution)/shard_map/ppermute | solution.py:30
  18.8 6.9 %collective-permute-start.6 = (s32[1,2]{0,1:T(2,128)S(1)}, s32[1,2]{0,1:T(2,128)S(1)}, u32[]{:S(2)}, u32[]{:S(2)}) collective-permute-start(s32[1,2]{0,1:T(2,128)S(1)} %get-tuple-element.22), channel_id=1, source_target_pairs={{0,28},{4,24},{8,20},{12,16},{16,12},{20,8},{24,4},{28,0},{1,29},{... | collective-permute-start | bytes 32 | tf_op jit(solution)/shard_map/ppermute | solution.py:30
  20.0 6.3 %collective-permute-start = (s32[1,2]{0,1:T(2,128)S(1)}, s32[1,2]{0,1:T(2,128)S(1)}, u32[]{:S(2)}, u32[]{:S(2)}) collective-permute-start(s32[1,2]{0,1:T(2,128)S(1)} %get-tuple-element.28), channel_id=1, source_target_pairs={{0,4},{4,0},{8,12},{12,8},{16,20},{20,16},{24,28},{28,24},{1,5},{5... | collective-permute-start | bytes 32 | tf_op jit(solution)/shard_map/ppermute | solution.py:30
  20.4 6.0 %collective-permute-start.1 = (s32[1,2]{0,1:T(2,128)S(1)}, s32[1,2]{0,1:T(2,128)S(1)}, u32[]{:S(2)}, u32[]{:S(2)}) collective-permute-start(s32[1,2]{0,1:T(2,128)S(1)} %get-tuple-element.27), channel_id=1, source_target_pairs={{0,8},{4,12},{8,0},{12,4},{16,24},{20,28},{24,16},{28,20},{1,9},{5... | collective-permute-start | bytes 32 | tf_op jit(solution)/shard_map/ppermute | solution.py:30
  20.4 6.0 %collective-permute-start.2 = (s32[1,2]{0,1:T(2,128)S(1)}, s32[1,2]{0,1:T(2,128)S(1)}, u32[]{:S(2)}, u32[]{:S(2)}) collective-permute-start(s32[1,2]{0,1:T(2,128)S(1)} %get-tuple-element.26), channel_id=1, source_target_pairs={{0,12},{4,8},{8,4},{12,0},{16,28},{20,24},{24,20},{28,16},{1,13},{... | collective-permute-start | bytes 32 | tf_op jit(solution)/shard_map/ppermute | solution.py:30
  23.5 4.5 %collective-permute-start.3 = (s32[1,2]{0,1:T(2,128)S(1)}, s32[1,2]{0,1:T(2,128)S(1)}, u32[]{:S(2)}, u32[]{:S(2)}) collective-permute-start(s32[1,2]{0,1:T(2,128)S(1)} %get-tuple-element.25), channel_id=1, source_target_pairs={{0,16},{4,20},{8,24},{12,28},{16,0},{20,4},{24,8},{28,12},{1,17},{... | collective-permute-start | bytes 32 | tf_op jit(solution)/shard_map/ppermute | solution.py:30
  25.7 5.4 %collective-permute-start.4 = (s32[1,2]{0,1:T(2,128)S(1)}, s32[1,2]{0,1:T(2,128)S(1)}, u32[]{:S(2)}, u32[]{:S(2)}) collective-permute-start(s32[1,2]{0,1:T(2,128)S(1)} %get-tuple-element.24), channel_id=1, source_target_pairs={{0,20},{4,16},{8,28},{12,24},{16,4},{20,0},{24,12},{28,8},{1,21},{... | collective-permute-start | bytes 32 | tf_op jit(solution)/shard_map/ppermute | solution.py:30
  42.8 95.5 %all-to-all-start = ((bf16[2,16,128,512]{3,2,0,1:T(8,128)(2,1)}), bf16[2,16,128,512]{3,2,0,1:T(8,128)(2,1)}, u32[]{:S(2)}, u32[]{:S(2)}) async-start(bf16[2,16,128,512]{3,2,0,1:T(8,128)(2,1)} %select_bitcast_fusion), calls=%async_computation | async-start | bytes 8388608 | tf_op jit(solution)/shard_map/all_to_all | solution.py:100
  47.4 25.6 %all-gather.2.cloned.1.call-start = ((), (), s32[]{:S(2)}) async-start(), calls=%async_computation.2 | async-start | bytes 2457600 | tf_op jit(solution)/shard_map/all_gather | solution.py:54
  48.1 168.8 %reduce-scatter.2.cloned.1.call-start = ((), (), s32[]{:S(2)}) async-start(), calls=%async_computation.3 | async-start | bytes 2457600 | tf_op jit(solution)/shard_map/reduce_scatter | solution.py:123
  81.0 8.3 %copy-start.4 = (f32[4]{0:T(128)S(1)}, f32[4]{0:T(128)}, u32[]{:S(2)}) copy-start(f32[4]{0:T(128)} %param.10) | copy-start | bytes 52
  85.2 9.6 %collective-permute-start.7 = (bf16[2,128,512]{1,2,0:T(8,128)(2,1)}, bf16[2,128,512]{1,2,0:T(8,128)(2,1)}, u32[]{:S(2)}, u32[]{:S(2)}) collective-permute-start(bf16[2,128,512]{1,2,0:T(8,128)(2,1)} %pad_maximum_fusion), channel_id=1, source_target_pairs={{0,4},{4,8},{8,12},{12,16},{16,20},{20,24},{24,28},{1,5},{5,9},{9,... | collective-permute-start | bytes 786440 | tf_op jit(solution)/shard_map/ppermute | solution.py:38
  96.0 1.7 copy-start.3
  146.9 4.0 %copy-start.2 = (bf16[384,4,1,128]{3,0,1,2:T(8,128)(2,1)S(1)}, bf16[384,4,1,128]{3,0,1,2:T(8,128)(2,1)}, u32[]{:S(2)}) copy-start(bf16[384,4,1,128]{3,0,1,2:T(8,128)(2,1)} %copy.92) | copy-start | bytes 1179652
  154.3 6.9 %copy-start.1 = (bf16[2048,4,128]{2,1,0:T(4,128)(2,1)S(1)}, bf16[2048,4,128]{2,1,0:T(4,128)(2,1)}, u32[]{:S(2)}) copy-start(bf16[2048,4,128]{2,1,0:T(4,128)(2,1)} %reshape.464) | copy-start | bytes 6291460
  161.2 9.3 %copy-start.5 = (f32[4,384]{1,0:T(4,128)S(1)}, f32[4,384]{1,0:T(4,128)}, u32[]{:S(2)}) copy-start(f32[4,384]{1,0:T(4,128)} %get-tuple-element.30) | copy-start | bytes 18436
Sparse Core Ops, SparseCore 0:
  49.8 23.1 all-gather.1
  175.9 40.9 reduce-scatter.1
